TPU v7x, 32 devices: a whole 2x2x4 slice. The times are simulated.
32 devices in a mesh: gx: 8 (over z, x), gy: 4 (over y, core).
Axes of the slice: x: 2, y: 2, z: 4, core: 2. Of those that a mesh axis runs over, the one named last changes fastest.
Arguments:
- fields: bfloat16 [4, 64, 128, 256], P(None, 'gx', 'gy'), may hold values from -6 to 6
- rows_live: int32 [8], replicated, may hold values from 4 to 8, as said below
- cols_live: int32 [4], replicated, may hold values from 16 to 32, as said below
- weight: bfloat16 [32, 108], replicated, may hold values from -0.625 to 0.625
- bias: float32 [32], replicated, may hold values from -3 to 3
- grad_out: bfloat16 [32, 32, 64, 128], P('gy', 'gx'), may hold values from -0.0625 to 0.0625
Outputs:
- stem: bfloat16 [32, 32, 64, 128], P('gy', 'gx')
- weight_grad: float32 [32, 108], P('gy')
- bias_grad: float32 [32], P('gy')
Inputs may be any that keep to these rules, and one draw needn't show every extreme that they name: `rows_live`: every entry is even, and some entry equals 8. `cols_live`: every entry is even, and some entry equals 32.
All inputs are finite; a program needn't handle non-finite values.
Results may differ from a plain program's by a relative error of at most 0.0054.
Values may be sent and summed in bfloat16 or wider, within the bound.
No kernel may reach another device: no remote copies, remote signals or barrier semaphores. Data moves between devices by JAX's collectives and lax.ppermute only.
A program may use at most 64 MiB of HBM per device.

v0:
```python
import jax
import jax.numpy as jnp
from jax import lax
from jax.sharding import PartitionSpec as P


def from_behind(block, axis, distance):
    devices = range(lax.axis_size(axis))
    route = [(i - distance, i) for i in devices if i - distance in devices]
    return lax.ppermute(block, axis, route)


def extend(data, border, count, dim):
    length = data.shape[dim]
    border_wide = jnp.expand_dims(border, dim)
    joined = jnp.concatenate([jnp.zeros_like(border_wide), data], axis=dim)
    shape = [1] * joined.ndim
    shape[dim] = length + 1
    places = jnp.arange(length + 1, dtype=jnp.int32).reshape(shape)
    edge_at = length - count
    kept = jnp.where(places > edge_at, joined, jnp.zeros_like(joined))
    return jnp.where(places == edge_at, border_wide, kept)


def taps(padded, axes, halves):
    pieces = []
    for off_x in range(3):
        for off_y in range(3):
            for off_z in range(3):
                piece = padded
                for axis_no, offset, half in zip(axes, (off_x, off_y, off_z), halves):
                    piece = lax.slice_in_dim(piece, offset, offset + 2 * half - 1, 2, axis_no)
                pieces.append(piece)
    return pieces


def local(fields, rows_live, cols_live, weight, bias, grad_out):
    in_chans, cap_x, cap_y, depth = fields.shape
    half_x = cap_x // 2
    half_y = cap_y // 2
    half_z = depth // 2
    out_chans = weight.shape[0]
    tiles_y = lax.axis_size("gy")
    row_count = rows_live[lax.axis_index("gx")]
    above = from_behind(fields[:, cap_x - 1], "gx", 1)
    ext_rows = extend(fields, above, row_count, 1)
    row_ok = jnp.arange(half_x, dtype=jnp.int32) >= half_x - row_count // 2
    col_count = cols_live[lax.axis_index("gy")]
    beside = from_behind(ext_rows[:, :, cap_y - 1], "gy", 1)
    ext_full = extend(ext_rows, beside, col_count, 2)
    padded = jnp.pad(ext_full, ((0, 0), (0, 0), (0, 0), (1, 0)))
    patches = jnp.stack(taps(padded, (1, 2, 3), (half_x, half_y, half_z)), axis=1).reshape(
        in_chans * 27, -1
    )
    conv = jnp.dot(weight, patches, preferred_element_type=jnp.float32) + bias[:, None]
    col_ok = jnp.arange(half_y, dtype=jnp.int32) >= half_y - col_count // 2
    live = (row_ok[:, None] & col_ok[None, :]).reshape(1, half_x, half_y, 1)
    conv = conv.reshape(out_chans, half_x, half_y, half_z)
    pre_local = jnp.where(live, conv, 0.0).astype(jnp.bfloat16)
    regrouped = lax.all_to_all(pre_local, "gy", split_axis=0, concat_axis=2, tiled=True)
    pre_wide = regrouped.astype(jnp.float32)
    sigma = jax.nn.sigmoid(pre_wide)
    stem = (pre_wide * sigma).astype(jnp.bfloat16)
    wide_cols = jnp.arange(half_y, dtype=jnp.int32)[None, :] >= half_y - (cols_live // 2)[:, None]
    wide_live = row_ok.reshape(1, half_x, 1, 1) & wide_cols.reshape(1, 1, tiles_y * half_y, 1)
    slope = sigma * (1.0 + pre_wide * (1.0 - sigma))
    grad_pre = jnp.where(wide_live, grad_out.astype(jnp.float32) * slope, 0.0).astype(jnp.bfloat16)
    returned = lax.all_to_all(grad_pre, "gy", split_axis=2, concat_axis=0, tiled=True)
    flat = returned.reshape(out_chans, -1)
    weight_full = lax.dot_general(
        flat, patches, (((1,), (1,)), ((), ())), preferred_element_type=jnp.float32
    )
    bias_full = jnp.sum(flat.astype(jnp.float32), axis=1)
    weight_part, bias_part = (
        lax.psum_scatter(weight_full, "gy", scatter_dimension=0, tiled=True),
        lax.psum_scatter(bias_full, "gy", scatter_dimension=0, tiled=True),
    )
    weight_grad, bias_grad = lax.psum((weight_part, bias_part), "gx")
    return (stem, weight_grad, bias_grad)


def solution(mesh):
    in_specs = (P(None, "gx", "gy", None), P(), P(), P(), P(), P("gy", "gx", None, None))
    out_specs = (P("gy", "gx", None, None), P("gy", None), P("gy"))
    return jax.shard_map(local, mesh=mesh, in_specs=in_specs, out_specs=out_specs, check_vma=False)
```

profile of v0, /device:TPU:0, one launch (start us, length us, event | category | flops | bytes accessed | tf_op | source)
XLA Modules:
  0.0 160.4 jit_solution(18269219123622887395)
XLA Ops:
  1.5 4.9 %collective-permute-start = (bf16[4,32,256]{2,1,0:T(8,128)(2,1)S(1)}, bf16[4,32,256]{2,1,0:T(8,128)(2,1)S(1)}, u32[]{:S(2)}, u32[]{:S(2)}) collective-permute-start(bf16[4,32,256]{2,1,0:T(8,128)(2,1)S(1)} %slice_bitcast_fusion), channel_id=1, source_target_pairs={{0,4},{4,8},{8,12},{12,16},{16,20},{20,24},{24,28},{1,5},{5,9},{9,... | collective-permute-start | bytes 196616 | tf_op jit(solution)/shard_map/ppermute | solution.py:10
  21.1 2.5 %slice.205 = bf16[4,4,16,128]{3,2,1,0:T(8,128)(2,1)S(1)} slice(bf16[4,4,16,257]{3,2,1,0:T(8,128)(2,1)S(1)} %slice.202), slice={[0:4:1], [0:4:1], [0:16:1], [2:257:2]} | slice | bytes 131072 | tf_op jit(solution)/shard_map/slice | solution.py:32
  23.7 2.5 %slice.204 = bf16[4,4,16,128]{3,2,1,0:T(8,128)(2,1)S(1)} slice(bf16[4,4,16,257]{3,2,1,0:T(8,128)(2,1)S(1)} %slice.202), slice={[0:4:1], [0:4:1], [0:16:1], [1:256:2]} | slice | bytes 131072 | tf_op jit(solution)/shard_map/slice | solution.py:32
  29.4 2.5 %slice.197 = bf16[4,4,16,128]{3,2,1,0:T(8,128)(2,1)S(1)} slice(bf16[4,4,16,257]{3,2,1,0:T(8,128)(2,1)S(1)} %slice.194), slice={[0:4:1], [0:4:1], [0:16:1], [2:257:2]} | slice | bytes 131072 | tf_op jit(solution)/shard_map/slice | solution.py:32
  31.9 2.5 %slice.196 = bf16[4,4,16,128]{3,2,1,0:T(8,128)(2,1)S(1)} slice(bf16[4,4,16,257]{3,2,1,0:T(8,128)(2,1)S(1)} %slice.194), slice={[0:4:1], [0:4:1], [0:16:1], [1:256:2]} | slice | bytes 131072 | tf_op jit(solution)/shard_map/slice | solution.py:32
  34.5 2.5 %slice.195 = bf16[4,4,16,128]{3,2,1,0:T(8,128)(2,1)S(1)} slice(bf16[4,4,16,257]{3,2,1,0:T(8,128)(2,1)S(1)} %slice.194), slice={[0:4:1], [0:4:1], [0:16:1], [0:255:2]} | slice | bytes 131072 | tf_op jit(solution)/shard_map/slice | solution.py:32
  37.0 2.5 %slice.201 = bf16[4,4,16,128]{3,2,1,0:T(8,128)(2,1)S(1)} slice(bf16[4,4,16,257]{3,2,1,0:T(8,128)(2,1)S(1)} %slice.198), slice={[0:4:1], [0:4:1], [0:16:1], [2:257:2]} | slice | bytes 131072 | tf_op jit(solution)/shard_map/slice | solution.py:32
  39.6 2.5 %slice.200 = bf16[4,4,16,128]{3,2,1,0:T(8,128)(2,1)S(1)} slice(bf16[4,4,16,257]{3,2,1,0:T(8,128)(2,1)S(1)} %slice.198), slice={[0:4:1], [0:4:1], [0:16:1], [1:256:2]} | slice | bytes 131072 | tf_op jit(solution)/shard_map/slice | solution.py:32
  42.1 2.5 %slice.199 = bf16[4,4,16,128]{3,2,1,0:T(8,128)(2,1)S(1)} slice(bf16[4,4,16,257]{3,2,1,0:T(8,128)(2,1)S(1)} %slice.198), slice={[0:4:1], [0:4:1], [0:16:1], [0:255:2]} | slice | bytes 131072 | tf_op jit(solution)/shard_map/slice | solution.py:32
  45.0 2.5 %slice.192 = bf16[4,4,16,128]{3,2,1,0:T(8,128)(2,1)S(1)} slice(bf16[4,4,16,257]{3,2,1,0:T(8,128)(2,1)S(1)} %slice.189), slice={[0:4:1], [0:4:1], [0:16:1], [2:257:2]} | slice | bytes 131072 | tf_op jit(solution)/shard_map/slice | solution.py:32
  47.5 2.5 %slice.191 = bf16[4,4,16,128]{3,2,1,0:T(8,128)(2,1)S(1)} slice(bf16[4,4,16,257]{3,2,1,0:T(8,128)(2,1)S(1)} %slice.189), slice={[0:4:1], [0:4:1], [0:16:1], [1:256:2]} | slice | bytes 131072 | tf_op jit(solution)/shard_map/slice | solution.py:32
  53.2 2.5 %slice.184 = bf16[4,4,16,128]{3,2,1,0:T(8,128)(2,1)S(1)} slice(bf16[4,4,16,257]{3,2,1,0:T(8,128)(2,1)S(1)} %slice.181), slice={[0:4:1], [0:4:1], [0:16:1], [2:257:2]} | slice | bytes 131072 | tf_op jit(solution)/shard_map/slice | solution.py:32
  55.8 2.5 %slice.183 = bf16[4,4,16,128]{3,2,1,0:T(8,128)(2,1)S(1)} slice(bf16[4,4,16,257]{3,2,1,0:T(8,128)(2,1)S(1)} %slice.181), slice={[0:4:1], [0:4:1], [0:16:1], [1:256:2]} | slice | bytes 131072 | tf_op jit(solution)/shard_map/slice | solution.py:32
  60.9 2.5 %slice.188 = bf16[4,4,16,128]{3,2,1,0:T(8,128)(2,1)S(1)} slice(bf16[4,4,16,257]{3,2,1,0:T(8,128)(2,1)S(1)} %slice.185), slice={[0:4:1], [0:4:1], [0:16:1], [2:257:2]} | slice | bytes 131072 | tf_op jit(solution)/shard_map/slice | solution.py:32
  68.9 2.5 %slice.179 = bf16[4,4,16,128]{3,2,1,0:T(8,128)(2,1)S(1)} slice(bf16[4,4,16,257]{3,2,1,0:T(8,128)(2,1)S(1)} %slice.176), slice={[0:4:1], [0:4:1], [0:16:1], [2:257:2]} | slice | bytes 131072 | tf_op jit(solution)/shard_map/slice | solution.py:32
  77.1 2.7 %slice.171 = bf16[4,4,16,128]{3,2,1,0:T(8,128)(2,1)S(1)} slice(bf16[4,4,16,257]{3,2,1,0:T(8,128)(2,1)S(1)} %slice.168), slice={[0:4:1], [0:4:1], [0:16:1], [2:257:2]} | slice | bytes 131072 | tf_op jit(solution)/shard_map/slice | solution.py:32
  84.9 2.5 %slice.175 = bf16[4,4,16,128]{3,2,1,0:T(8,128)(2,1)S(1)} slice(bf16[4,4,16,257]{3,2,1,0:T(8,128)(2,1)S(1)} %slice.172), slice={[0:4:1], [0:4:1], [0:16:1], [2:257:2]} | slice | bytes 131072 | tf_op jit(solution)/shard_map/slice | solution.py:32
  94.6 2.7 %reshape.144 = bf16[108,8192]{1,0:T(8,128)(2,1)S(1)} reshape(bf16[4,27,4,16,128]{4,3,2,1,0:T(8,128)(2,1)} %copy.24) | data formatting | bytes 3538944 | tf_op jit(solution)/shard_map/reshape | solution.py:52
  98.9 5.6 %all-to-all-start = ((bf16[32,4,16,128]{3,2,1,0:T(8,128)(2,1)}), bf16[32,4,16,128]{3,2,1,0:T(8,128)(2,1)S(1)}, u32[]{:S(2)}, u32[]{:S(2)}) async-start(bf16[32,4,16,128]{3,2,1,0:T(8,128)(2,1)} %select_convert_fusion), calls=%async_computation | async-start | bytes 1048576 | tf_op jit(solution)/shard_map/all_to_all | solution.py:60
  104.7 8.6 %all-to-all-done = bf16[32,4,16,128]{3,2,1,0:T(8,128)(2,1)S(1)} async-done(((bf16[32,4,16,128]{3,2,1,0:T(8,128)(2,1)}), bf16[32,4,16,128]{3,2,1,0:T(8,128)(2,1)S(1)}, u32[]{:S(2)}, u32[]{:S(2)}) %all-to-all-start) | async-done | bytes 524320 | tf_op jit(solution)/shard_map/all_to_all | solution.py:60
  116.0 3.5 %all-to-all-start.1 = ((bf16[8,4,64,128]{3,0,1,2:T(8,128)(2,1)}), bf16[8,4,64,128]{3,0,1,2:T(8,128)(2,1)S(1)}, u32[]{:S(2)}, u32[]{:S(2)}) async-start(bf16[8,4,64,128]{3,0,1,2:T(8,128)(2,1)} %get-tuple-element.13), calls=%async_computation.1 | async-start | bytes 1048576 | tf_op jit(solution)/shard_map/all_to_all | solution.py:68
  121.7 6.5 %all-to-all-done.1 = bf16[8,4,64,128]{3,0,1,2:T(8,128)(2,1)S(1)} async-done(((bf16[8,4,64,128]{3,0,1,2:T(8,128)(2,1)}), bf16[8,4,64,128]{3,0,1,2:T(8,128)(2,1)S(1)}, u32[]{:S(2)}, u32[]{:S(2)}) %all-to-all-start.1) | async-done | bytes 524320 | tf_op jit(solution)/shard_map/all_to_all | solution.py:68
  129.8 10.3 %all-reduce.6 = (f32[32,108]{1,0:T(8,128)S(1)}, f32[32]{0:T(128)S(1)}) all-reduce(f32[32,108]{1,0:T(8,128)S(1)} %fusion.11, f32[32]{0:T(128)S(1)} %reduce_sum.12), channel_id=2, replica_groups=mesh['gx'=8,'gy'=4] {'gy'}, use_global_device_ids=true, to_apply=%region_0.1.clone | all-reduce | flops 3488 | bytes 27904
  140.1 20.3 %all-reduce.5 = (f32[8,108]{1,0:T(8,128)}, f32[8]{0:T(128)}) all-reduce(f32[8,108]{1,0:T(8,128)S(1)} %constant_dynamic-slice_fusion, f32[8]{0:T(128)S(1)} %dynamic-slice.3), channel_id=1, replica_groups=mesh['gx'=8,'gy'=4] {'gx'}, use_global_device_ids=true, to_apply=%region_1.2 | all-reduce | flops 872 | bytes 6976 | tf_op jit(solution)/shard_map/psum | solution.py:78
  (91 shorter events, 48.9 us)
Async XLA Ops:
  0.6 96.7 %copy-start = (bf16[32,108]{1,0:T(8,128)(2,1)S(1)}, bf16[32,108]{1,0:T(8,128)(2,1)}, u32[]{:S(2)}) copy-start(bf16[32,108]{1,0:T(8,128)(2,1)} %param.9) | copy-start | bytes 20740
  1.5 14.7 %collective-permute-start = (bf16[4,32,256]{2,1,0:T(8,128)(2,1)S(1)}, bf16[4,32,256]{2,1,0:T(8,128)(2,1)S(1)}, u32[]{:S(2)}, u32[]{:S(2)}) collective-permute-start(bf16[4,32,256]{2,1,0:T(8,128)(2,1)S(1)} %slice_bitcast_fusion), channel_id=1, source_target_pairs={{0,4},{4,8},{8,12},{12,16},{16,20},{20,24},{24,28},{1,5},{5,9},{9,... | collective-permute-start | bytes 196616 | tf_op jit(solution)/shard_map/ppermute | solution.py:10
  17.4 2.3 %collective-permute-start.1 = (bf16[4,9,256]{2,0,1:T(4,128)(2,1)S(1)}, bf16[4,9,256]{2,0,1:T(4,128)(2,1)S(1)}, u32[]{:S(2)}, u32[]{:S(2)}) collective-permute-start(bf16[4,9,256]{2,0,1:T(4,128)(2,1)S(1)} %bitcast.116), channel_id=1, source_target_pairs={{0,1},{1,2},{2,3},{4,5},{5,6},{6,7},{8,9},{9,10},{10,11},{12,13},{... | collective-permute-start | bytes 55304 | tf_op jit(solution)/shard_map/ppermute | solution.py:10
  94.6 2.7 %copy-start.2 = (f32[32]{0:T(128)S(1)}, f32[32]{0:T(128)}, u32[]{:S(2)}) copy-start(f32[32]{0:T(128)} %param.10) | copy-start | bytes 388
  97.9 15.7 %copy-start.1 = (bf16[8,4,64,128]{3,2,1,0:T(8,128)(2,1)S(1)}, bf16[8,4,64,128]{3,2,1,0:T(8,128)(2,1)}, u32[]{:S(2)}) copy-start(bf16[8,4,64,128]{3,2,1,0:T(8,128)(2,1)} %param.11) | copy-start | bytes 1572868
  98.9 14.4 %all-to-all-start = ((bf16[32,4,16,128]{3,2,1,0:T(8,128)(2,1)}), bf16[32,4,16,128]{3,2,1,0:T(8,128)(2,1)S(1)}, u32[]{:S(2)}, u32[]{:S(2)}) async-start(bf16[32,4,16,128]{3,2,1,0:T(8,128)(2,1)} %select_convert_fusion), calls=%async_computation | async-start | bytes 1048576 | tf_op jit(solution)/shard_map/all_to_all | solution.py:60
  113.6 5.9 %copy-start.3 = (u32[32]{0:T(128)S(1)}, u32[32]{0:T(128)}, u32[]{:S(2)}) copy-start(u32[32]{0:T(128)} %constant.68) | copy-start | bytes 388
  116.0 12.3 %all-to-all-start.1 = ((bf16[8,4,64,128]{3,0,1,2:T(8,128)(2,1)}), bf16[8,4,64,128]{3,0,1,2:T(8,128)(2,1)S(1)}, u32[]{:S(2)}, u32[]{:S(2)}) async-start(bf16[8,4,64,128]{3,0,1,2:T(8,128)(2,1)} %get-tuple-element.13), calls=%async_computation.1 | async-start | bytes 1048576 | tf_op jit(solution)/shard_map/all_to_all | solution.py:68
where the time goes:
time: 161 us; the launch traced here: 160 us
  local copies, waits for them, and re-layouts  82.8 us (51%)
  blocking collectives  30.6 us (19%)
  waiting for transfers between devices  15.9 us (10%)
  starting transfers between devices  15.4 us (10%)
  between operations  8.42 us (5%)
  other arithmetic  6.2 us (4%)
    slice x37, local copies, waits for them, and re-layouts, taps(): piece = lax.slice_in_dim(piece, offset, offset + 2 * half - 1, 2, axis_no)  72.1 us
    psum x1, blocking collectives, local(): weight_grad, bias_grad = lax.psum((weight_part, bias_part), 'gx')  20.3 us
    unnamed x1, blocking collectives  10.3 us
    all_to_all x1, waiting for transfers between devices, local(): lax.all_to_all(pre_local, 'gy', split_axis=0, concat_axis=2, tiled=True)  8.57 us
    all_to_all x1, waiting for transfers between devices, local(): lax.all_to_all(grad_pre, 'gy', split_axis=2, concat_axis=0, tiled=True)  6.53 us
    ppermute x2, starting transfers between devices, from_behind(): return lax.ppermute(block, axis, route)  6.32 us
    all_to_all x1, starting transfers between devices, local(): lax.all_to_all(pre_local, 'gy', split_axis=0, concat_axis=2, tiled=True)  5.58 us
    all_to_all x1, starting transfers between devices, local(): lax.all_to_all(grad_pre, 'gy', split_axis=2, concat_axis=0, tiled=True)  3.47 us
  transfers between devices with their start and end apart: 4, of which 3 were waited for; matrix products, arithmetic and copies ran while one was open for 3% of the time, Pallas kernels for 0%

commit v1 on v0

--- a/solution.py
+++ b/solution.py
@@ -2,6 +2,20 @@
 import jax.numpy as jnp
 from jax import lax
 from jax.sharding import PartitionSpec as P
+
+
+def _follow_slabs(my_data, array_axis, target):
+    near = my_data.shape
+    reply = my_data.reshape(
+        *near[:array_axis], target, near[array_axis] // target, *near[array_axis + 1 :]
+    )
+    return jnp.moveaxis(reply, array_axis, 0)
+
+
+def axis_part_state(mat, out_dim):
+    mat = jnp.moveaxis(mat, 0, out_dim)
+    top = mat.shape
+    return mat.reshape(*top[:out_dim], top[out_dim] * top[out_dim + 1], *top[out_dim + 2 :])
 
 
 def from_behind(block, axis, distance):
@@ -65,7 +79,18 @@
     wide_live = row_ok.reshape(1, half_x, 1, 1) & wide_cols.reshape(1, 1, tiles_y * half_y, 1)
     slope = sigma * (1.0 + pre_wide * (1.0 - sigma))
     grad_pre = jnp.where(wide_live, grad_out.astype(jnp.float32) * slope, 0.0).astype(jnp.bfloat16)
-    returned = lax.all_to_all(grad_pre, "gy", split_axis=2, concat_axis=0, tiled=True)
+    w1, a_now = (lax.axis_size("gy"), lax.axis_index("gy"))
+    state_next = _follow_slabs(grad_pre, 2, w1)
+    tall = state_next
+    for k0 in tuple(range(1, w1)):
+        f_now, carry_out = ((a_now + k0) % w1, (a_now - k0) % w1)
+        piece_next = lax.dynamic_index_in_dim(state_next, f_now, 0)
+        chunks = []
+        for tick in tuple(range(w1)):
+            chunks.append((tick, (tick + k0) % w1))
+        t_next = lax.ppermute(piece_next, axis_name="gy", perm=chunks)
+        tall = lax.dynamic_update_slice_in_dim(tall, t_next, carry_out, axis=0)
+    returned = axis_part_state(tall, 0)
     flat = returned.reshape(out_chans, -1)
     weight_full = lax.dot_general(
         flat, patches, (((1,), (1,)), ((), ())), preferred_element_type=jnp.float32

time: 161 us -> 156 us (0.969)
  waiting for transfers between devices: 15.9 us -> 12.6 us
  blocking collectives: 30.6 us -> 32.3 us
    all_to_all x1 -> x0, waiting for transfers between devices: 6.53 us -> none  [local(): lax.all_to_all(grad_pre, 'gy', split_axis=2, concat_axis=0, tiled=True)]
    all_to_all x1 -> x0, starting transfers between devices: 3.47 us -> none  [local(): lax.all_to_all(grad_pre, 'gy', split_axis=2, concat_axis=0, tiled=True)]
    ppermute x0 -> x3, waiting for transfers between devices: none -> 3.26 us  [local(): t_next = lax.ppermute(piece_next, axis_name='gy', perm=chunks)]
    ppermute x0 -> x3, starting transfers between devices: none -> 1.96 us  [local(): t_next = lax.ppermute(piece_next, axis_name='gy', perm=chunks)]
    unnamed x1, blocking collectives: 10.3 us -> 12 us
  transfers between devices with their start and end apart: 4 -> 6, of which waited for: 3 -> 4; matrix products, arithmetic and copies ran while one was open for 3% -> 3% of each run, Pallas kernels for 0% -> 0%
where the time goes in v1:
time: 156 us; the launch traced here: 155 us
  local copies, waits for them, and re-layouts  81.6 us (52%)
  blocking collectives  32.3 us (21%)
  starting transfers between devices  13.9 us (9%)
  waiting for transfers between devices  12.6 us (8%)
  between operations  8.47 us (5%)
  other arithmetic  5.12 us (3%)
    slice x37, local copies, waits for them, and re-layouts, taps(): piece = lax.slice_in_dim(piece, offset, offset + 2 * half - 1, 2, axis_no)  72.1 us
    psum x1, blocking collectives, local(): weight_grad, bias_grad = lax.psum((weight_part, bias_part), 'gx')  20.3 us
    unnamed x1, blocking collectives  12 us
    all_to_all x1, waiting for transfers between devices, local(): lax.all_to_all(pre_local, 'gy', split_axis=0, concat_axis=2, tiled=True)  8.57 us
    ppermute x2, starting transfers between devices, from_behind(): return lax.ppermute(block, axis, route)  6.32 us
    all_to_all x1, starting transfers between devices, local(): lax.all_to_all(pre_local, 'gy', split_axis=0, concat_axis=2, tiled=True)  5.58 us
    ppermute x3, waiting for transfers between devices, local(): t_next = lax.ppermute(piece_next, axis_name='gy', perm=chunks)  3.26 us
  transfers between devices with their start and end apart: 6, of which 4 were waited for; matrix products, arithmetic and copies ran while one was open for 3% of the time, Pallas kernels for 0%

profile of v1, /device:TPU:0, one launch (start us, length us, event | category | flops | bytes accessed | tf_op | source)
XLA Modules:
  0.0 155.1 jit_solution(14247870315032474354)
XLA Ops:
  1.5 4.9 %collective-permute-start = (bf16[4,32,256]{2,1,0:T(8,128)(2,1)S(1)}, bf16[4,32,256]{2,1,0:T(8,128)(2,1)S(1)}, u32[]{:S(2)}, u32[]{:S(2)}) collective-permute-start(bf16[4,32,256]{2,1,0:T(8,128)(2,1)S(1)} %slice_bitcast_fusion), channel_id=1, source_target_pairs={{0,4},{4,8},{8,12},{12,16},{16,20},{20,24},{24,28},{1,5},{5,9},{9,... | collective-permute-start | bytes 196616 | tf_op jit(solution)/shard_map/ppermute | solution.py:24
  21.1 2.5 %slice.205 = bf16[4,4,16,128]{3,2,1,0:T(8,128)(2,1)S(1)} slice(bf16[4,4,16,257]{3,2,1,0:T(8,128)(2,1)S(1)} %slice.202), slice={[0:4:1], [0:4:1], [0:16:1], [2:257:2]} | slice | bytes 131072 | tf_op jit(solution)/shard_map/slice | solution.py:46
  23.7 2.5 %slice.204 = bf16[4,4,16,128]{3,2,1,0:T(8,128)(2,1)S(1)} slice(bf16[4,4,16,257]{3,2,1,0:T(8,128)(2,1)S(1)} %slice.202), slice={[0:4:1], [0:4:1], [0:16:1], [1:256:2]} | slice | bytes 131072 | tf_op jit(solution)/shard_map/slice | solution.py:46
  29.4 2.5 %slice.197 = bf16[4,4,16,128]{3,2,1,0:T(8,128)(2,1)S(1)} slice(bf16[4,4,16,257]{3,2,1,0:T(8,128)(2,1)S(1)} %slice.194), slice={[0:4:1], [0:4:1], [0:16:1], [2:257:2]} | slice | bytes 131072 | tf_op jit(solution)/shard_map/slice | solution.py:46
  31.9 2.5 %slice.196 = bf16[4,4,16,128]{3,2,1,0:T(8,128)(2,1)S(1)} slice(bf16[4,4,16,257]{3,2,1,0:T(8,128)(2,1)S(1)} %slice.194), slice={[0:4:1], [0:4:1], [0:16:1], [1:256:2]} | slice | bytes 131072 | tf_op jit(solution)/shard_map/slice | solution.py:46
  34.5 2.5 %slice.195 = bf16[4,4,16,128]{3,2,1,0:T(8,128)(2,1)S(1)} slice(bf16[4,4,16,257]{3,2,1,0:T(8,128)(2,1)S(1)} %slice.194), slice={[0:4:1], [0:4:1], [0:16:1], [0:255:2]} | slice | bytes 131072 | tf_op jit(solution)/shard_map/slice | solution.py:46
  37.0 2.5 %slice.201 = bf16[4,4,16,128]{3,2,1,0:T(8,128)(2,1)S(1)} slice(bf16[4,4,16,257]{3,2,1,0:T(8,128)(2,1)S(1)} %slice.198), slice={[0:4:1], [0:4:1], [0:16:1], [2:257:2]} | slice | bytes 131072 | tf_op jit(solution)/shard_map/slice | solution.py:46
  39.6 2.5 %slice.200 = bf16[4,4,16,128]{3,2,1,0:T(8,128)(2,1)S(1)} slice(bf16[4,4,16,257]{3,2,1,0:T(8,128)(2,1)S(1)} %slice.198), slice={[0:4:1], [0:4:1], [0:16:1], [1:256:2]} | slice | bytes 131072 | tf_op jit(solution)/shard_map/slice | solution.py:46
  42.1 2.5 %slice.199 = bf16[4,4,16,128]{3,2,1,0:T(8,128)(2,1)S(1)} slice(bf16[4,4,16,257]{3,2,1,0:T(8,128)(2,1)S(1)} %slice.198), slice={[0:4:1], [0:4:1], [0:16:1], [0:255:2]} | slice | bytes 131072 | tf_op jit(solution)/shard_map/slice | solution.py:46
  45.0 2.5 %slice.192 = bf16[4,4,16,128]{3,2,1,0:T(8,128)(2,1)S(1)} slice(bf16[4,4,16,257]{3,2,1,0:T(8,128)(2,1)S(1)} %slice.189), slice={[0:4:1], [0:4:1], [0:16:1], [2:257:2]} | slice | bytes 131072 | tf_op jit(solution)/shard_map/slice | solution.py:46
  47.5 2.5 %slice.191 = bf16[4,4,16,128]{3,2,1,0:T(8,128)(2,1)S(1)} slice(bf16[4,4,16,257]{3,2,1,0:T(8,128)(2,1)S(1)} %slice.189), slice={[0:4:1], [0:4:1], [0:16:1], [1:256:2]} | slice | bytes 131072 | tf_op jit(solution)/shard_map/slice | solution.py:46
  53.2 2.5 %slice.184 = bf16[4,4,16,128]{3,2,1,0:T(8,128)(2,1)S(1)} slice(bf16[4,4,16,257]{3,2,1,0:T(8,128)(2,1)S(1)} %slice.181), slice={[0:4:1], [0:4:1], [0:16:1], [2:257:2]} | slice | bytes 131072 | tf_op jit(solution)/shard_map/slice | solution.py:46
  55.8 2.5 %slice.183 = bf16[4,4,16,128]{3,2,1,0:T(8,128)(2,1)S(1)} slice(bf16[4,4,16,257]{3,2,1,0:T(8,128)(2,1)S(1)} %slice.181), slice={[0:4:1], [0:4:1], [0:16:1], [1:256:2]} | slice | bytes 131072 | tf_op jit(solution)/shard_map/slice | solution.py:46
  58.3 2.5 %slice.182 = bf16[4,4,16,128]{3,2,1,0:T(8,128)(2,1)S(1)} slice(bf16[4,4,16,257]{3,2,1,0:T(8,128)(2,1)S(1)} %slice.181), slice={[0:4:1], [0:4:1], [0:16:1], [0:255:2]} | slice | bytes 131072 | tf_op jit(solution)/shard_map/slice | solution.py:46
  60.9 2.5 %slice.188 = bf16[4,4,16,128]{3,2,1,0:T(8,128)(2,1)S(1)} slice(bf16[4,4,16,257]{3,2,1,0:T(8,128)(2,1)S(1)} %slice.185), slice={[0:4:1], [0:4:1], [0:16:1], [2:257:2]} | slice | bytes 131072 | tf_op jit(solution)/shard_map/slice | solution.py:46
  63.4 2.5 %slice.187 = bf16[4,4,16,128]{3,2,1,0:T(8,128)(2,1)S(1)} slice(bf16[4,4,16,257]{3,2,1,0:T(8,128)(2,1)S(1)} %slice.185), slice={[0:4:1], [0:4:1], [0:16:1], [1:256:2]} | slice | bytes 131072 | tf_op jit(solution)/shard_map/slice | solution.py:46
  68.9 2.5 %slice.179 = bf16[4,4,16,128]{3,2,1,0:T(8,128)(2,1)S(1)} slice(bf16[4,4,16,257]{3,2,1,0:T(8,128)(2,1)S(1)} %slice.176), slice={[0:4:1], [0:4:1], [0:16:1], [2:257:2]} | slice | bytes 131072 | tf_op jit(solution)/shard_map/slice | solution.py:46
  77.1 2.7 %slice.171 = bf16[4,4,16,128]{3,2,1,0:T(8,128)(2,1)S(1)} slice(bf16[4,4,16,257]{3,2,1,0:T(8,128)(2,1)S(1)} %slice.168), slice={[0:4:1], [0:4:1], [0:16:1], [2:257:2]} | slice | bytes 131072 | tf_op jit(solution)/shard_map/slice | solution.py:46
  84.9 2.5 %slice.175 = bf16[4,4,16,128]{3,2,1,0:T(8,128)(2,1)S(1)} slice(bf16[4,4,16,257]{3,2,1,0:T(8,128)(2,1)S(1)} %slice.172), slice={[0:4:1], [0:4:1], [0:16:1], [2:257:2]} | slice | bytes 131072 | tf_op jit(solution)/shard_map/slice | solution.py:46
  94.6 2.7 %reshape.146 = bf16[108,8192]{1,0:T(8,128)(2,1)S(1)} reshape(bf16[4,27,4,16,128]{4,3,2,1,0:T(8,128)(2,1)} %copy.17) | data formatting | bytes 3538944 | tf_op jit(solution)/shard_map/reshape | solution.py:66
  98.9 5.6 %all-to-all-start = ((bf16[32,4,16,128]{3,2,1,0:T(8,128)(2,1)}), bf16[32,4,16,128]{3,2,1,0:T(8,128)(2,1)S(1)}, u32[]{:S(2)}, u32[]{:S(2)}) async-start(bf16[32,4,16,128]{3,2,1,0:T(8,128)(2,1)} %select_convert_fusion), calls=%async_computation | async-start | bytes 1048576 | tf_op jit(solution)/shard_map/all_to_all | solution.py:74
  104.7 8.6 %all-to-all-done = bf16[32,4,16,128]{3,2,1,0:T(8,128)(2,1)S(1)} async-done(((bf16[32,4,16,128]{3,2,1,0:T(8,128)(2,1)}), bf16[32,4,16,128]{3,2,1,0:T(8,128)(2,1)S(1)}, u32[]{:S(2)}, u32[]{:S(2)}) %all-to-all-start) | async-done | bytes 524320 | tf_op jit(solution)/shard_map/all_to_all | solution.py:74
  122.7 12.0 %all-reduce.6 = (f32[32,108]{1,0:T(8,128)S(1)}, f32[32]{0:T(128)S(1)}) all-reduce(f32[32,108]{1,0:T(8,128)S(1)} %fusion.11, f32[32]{0:T(128)S(1)} %reduce_sum.12), channel_id=2, replica_groups=mesh['gx'=8,'gy'=4] {'gy'}, use_global_device_ids=true, to_apply=%region_0.1.clone | all-reduce | flops 3488 | bytes 27904
  134.7 20.3 %all-reduce.5 = (f32[8,108]{1,0:T(8,128)}, f32[8]{0:T(128)}) all-reduce(f32[8,108]{1,0:T(8,128)S(1)} %constant_dynamic-slice_fusion, f32[8]{0:T(128)S(1)} %dynamic-slice.15), channel_id=1, replica_groups=mesh['gx'=8,'gy'=4] {'gx'}, use_global_device_ids=true, to_apply=%region_1.2 | all-reduce | flops 872 | bytes 6976 | tf_op jit(solution)/shard_map/psum | solution.py:103
  (98 shorter events, 46.7 us)
Async XLA Ops:
  0.6 96.7 %copy-start = (bf16[32,108]{1,0:T(8,128)(2,1)S(1)}, bf16[32,108]{1,0:T(8,128)(2,1)}, u32[]{:S(2)}) copy-start(bf16[32,108]{1,0:T(8,128)(2,1)} %param.9) | copy-start | bytes 20740
  1.5 14.7 %collective-permute-start = (bf16[4,32,256]{2,1,0:T(8,128)(2,1)S(1)}, bf16[4,32,256]{2,1,0:T(8,128)(2,1)S(1)}, u32[]{:S(2)}, u32[]{:S(2)}) collective-permute-start(bf16[4,32,256]{2,1,0:T(8,128)(2,1)S(1)} %slice_bitcast_fusion), channel_id=1, source_target_pairs={{0,4},{4,8},{8,12},{12,16},{16,20},{20,24},{24,28},{1,5},{5,9},{9,... | collective-permute-start | bytes 196616 | tf_op jit(solution)/shard_map/ppermute | solution.py:24
  17.4 2.3 %collective-permute-start.1 = (bf16[4,9,256]{2,0,1:T(4,128)(2,1)S(1)}, bf16[4,9,256]{2,0,1:T(4,128)(2,1)S(1)}, u32[]{:S(2)}, u32[]{:S(2)}) collective-permute-start(bf16[4,9,256]{2,0,1:T(4,128)(2,1)S(1)} %bitcast.120), channel_id=1, source_target_pairs={{0,1},{1,2},{2,3},{4,5},{5,6},{6,7},{8,9},{9,10},{10,11},{12,13},{... | collective-permute-start | bytes 55304 | tf_op jit(solution)/shard_map/ppermute | solution.py:24
  94.6 2.7 %copy-start.2 = (f32[32]{0:T(128)S(1)}, f32[32]{0:T(128)}, u32[]{:S(2)}) copy-start(f32[32]{0:T(128)} %param.10) | copy-start | bytes 388
  97.9 15.5 %copy-start.1 = (bf16[8,4,64,128]{3,2,1,0:T(8,128)(2,1)S(1)}, bf16[8,4,64,128]{3,2,1,0:T(8,128)(2,1)}, u32[]{:S(2)}) copy-start(bf16[8,4,64,128]{3,2,1,0:T(8,128)(2,1)} %param.11) | copy-start | bytes 1572868
  98.9 14.4 %all-to-all-start = ((bf16[32,4,16,128]{3,2,1,0:T(8,128)(2,1)}), bf16[32,4,16,128]{3,2,1,0:T(8,128)(2,1)S(1)}, u32[]{:S(2)}, u32[]{:S(2)}) async-start(bf16[32,4,16,128]{3,2,1,0:T(8,128)(2,1)} %select_convert_fusion), calls=%async_computation | async-start | bytes 1048576 | tf_op jit(solution)/shard_map/all_to_all | solution.py:74
  113.4 1.9 %copy-start.3 = (u32[32]{0:T(128)S(1)}, u32[32]{0:T(128)}, u32[]{:S(2)}) copy-start(u32[32]{0:T(128)} %constant.114) | copy-start | bytes 388
  114.8 5.2 %collective-permute-start.2 = (bf16[1,8,4,16,128]{4,3,2,1,0:T(8,128)(2,1)S(1)}, bf16[1,8,4,16,128]{4,3,2,1,0:T(8,128)(2,1)S(1)}, u32[]{:S(2)}, u32[]{:S(2)}) collective-permute-start(bf16[1,8,4,16,128]{4,3,2,1,0:T(8,128)(2,1)S(1)} %get-tuple-element.14), channel_id=1, source_target_pairs={{0,1},{1,2},{2,3},{3,0},{4,5},{5,6},{6,7},{7,4},{8,9},{9,10},{10,1... | collective-permute-start | bytes 393224 | tf_op jit(solution)/shard_map/ppermute | solution.py:91
  114.9 6.4 %collective-permute-start.3 = (bf16[1,8,4,16,128]{4,3,2,1,0:T(8,128)(2,1)S(1)}, bf16[1,8,4,16,128]{4,3,2,1,0:T(8,128)(2,1)S(1)}, u32[]{:S(2)}, u32[]{:S(2)}) collective-permute-start(bf16[1,8,4,16,128]{4,3,2,1,0:T(8,128)(2,1)S(1)} %get-tuple-element.13), channel_id=1, source_target_pairs={{0,2},{1,3},{2,0},{3,1},{4,6},{5,7},{6,4},{7,5},{8,10},{9,11},{10,... | collective-permute-start | bytes 393224 | tf_op jit(solution)/shard_map/ppermute | solution.py:91
  116.7 4.7 %collective-permute-start.4 = (bf16[1,8,4,16,128]{4,3,2,1,0:T(8,128)(2,1)S(1)}, bf16[1,8,4,16,128]{4,3,2,1,0:T(8,128)(2,1)S(1)}, u32[]{:S(2)}, u32[]{:S(2)}) collective-permute-start(bf16[1,8,4,16,128]{4,3,2,1,0:T(8,128)(2,1)S(1)} %get-tuple-element.12), channel_id=1, source_target_pairs={{0,3},{1,0},{2,1},{3,2},{4,7},{5,4},{6,5},{7,6},{8,11},{9,8},{10,9... | collective-permute-start | bytes 393224 | tf_op jit(solution)/shard_map/ppermute | solution.py:91
